TPU v7x, 256 devices: a whole 4x4x8 slice. The times are simulated.
256 devices in a mesh: section: 8 (over x, core), expert: 32 (over z, y).
Axes of the slice: x: 4, y: 4, z: 8, core: 2. Of those that a mesh axis runs over, the one named last changes fastest.
Arguments:
- tokens: bfloat16 [8, 2304, 2048], P(None, 'expert'), may hold values from -6 to 6
- w_in: bfloat16 [8, 2048, 2048], P('section', 'expert'), may hold values from -0.125 to 0.125
- w_out: bfloat16 [8, 2048, 2048], P('section', 'expert'), may hold values from -0.125 to 0.125
- router: bfloat16 [2048, 32], replicated, may hold values from -0.125 to 0.125
- exp_in: bfloat16 [32, 2048, 2048], P('expert', None, 'section'), may hold values from -0.125 to 0.125
- exp_out: bfloat16 [32, 2048, 2048], P('expert', 'section'), may hold values from -0.375 to 0.375
- active_rows: int32 [4608], P('expert'), may hold values from 0 to 575, as said below
- active_expert: int32 [4608, 1], P('expert'), may hold values from 0 to 31; in each aligned block of 144 rows (0 to 143, 144 to 287, ...) at most 13 rows name the same one
Outputs:
- updated: bfloat16 [8, 2304, 2048], P(None, 'expert', 'section')
Inputs may be any that keep to these rules, and one draw needn't show every extreme that they name: `active_rows`: the 144 entries of one token block name distinct rows of its 576 rows. `active_expert`: among the 144 entries of one token block no expert is named more than 13 times.
All inputs are finite; a program needn't handle non-finite values.
Results may differ from a plain program's by a relative error of at most 0.024.
Values may be sent and summed in bfloat16 or wider, within the bound.
No kernel may reach another device: no remote copies, remote signals or barrier semaphores. Data moves between devices by JAX's collectives and lax.ppermute only.
A program may use at most 64 MiB of HBM per device.

v0:
```python
import jax
import jax.numpy as jnp
from jax import lax
from jax.sharding import PartitionSpec as P


def from_behind(value, axis, steps):
    count = lax.axis_size(axis)
    initial, last = (max(0, -steps), min(count, count - steps))
    return lax.ppermute(value, axis, [(source, source + steps) for source in range(initial, last)])


def normalize(rows):
    wide = rows.astype(jnp.float32)
    scale = lax.rsqrt(jnp.mean(wide * wide, axis=-1, keepdims=True) + 1e-05)
    return wide * scale


def processor(stream, w_first, w_second):
    normed = normalize(stream).astype(jnp.bfloat16)
    hidden = jax.nn.silu(jnp.dot(normed, w_first, preferred_element_type=jnp.float32)).astype(
        jnp.bfloat16
    )
    branch = jnp.dot(hidden, w_second, preferred_element_type=jnp.float32)
    return (stream.astype(jnp.float32) + branch).astype(jnp.bfloat16)


def local(tokens, w_in, w_out, router, exp_in, exp_out, active_rows, active_expert):
    n_section = lax.axis_size("section")
    n_expert = lax.axis_size("expert")
    section = lax.axis_index("section")
    expert_index = lax.axis_index("expert")
    micro, tok_dev, width = tokens.shape
    w_first, w_second = (
        lax.all_gather(w_in, "expert", axis=1, tiled=True),
        lax.all_gather(w_out, "expert", axis=1, tiled=True),
    )
    w_first = w_first[0]
    w_second = w_second[0]
    last = n_section - 1

    def run_layer(stream):
        return processor(stream, w_first, w_second)

    def skip_layer(stream):
        return jnp.zeros_like(stream)

    def tick(step, carry):
        incoming, collected = carry
        micro_index = step - section
        valid = (micro_index >= 0) & (micro_index < micro)
        clamped = jnp.clip(micro_index, 0, micro - 1)
        fresh = lax.dynamic_index_in_dim(tokens, clamped, 0, keepdims=False)
        stream = jnp.where(section == 0, fresh, incoming)
        result = lax.cond(valid, run_layer, skip_layer, stream)
        updated = lax.dynamic_update_index_in_dim(collected, result, clamped, 0)
        collected = jnp.where(valid & (section == last), updated, collected)
        passed = from_behind(result, "section", 1)
        return (passed, collected)

    start = (jnp.zeros((tok_dev, width), jnp.bfloat16), jnp.zeros_like(tokens))
    passed, collected = lax.fori_loop(0, micro + n_section - 1, tick, start)
    rows_dev = micro * tok_dev
    flat = collected.reshape(rows_dev, width)
    n_exp = router.shape[1]
    part_width = width // n_section
    per_sub = 2
    ranks = n_section * per_sub
    chosen = active_expert[:, 0]
    onehot = chosen[:, None] == jnp.arange(n_exp, dtype=jnp.int32)[None, :]
    counts = onehot.astype(jnp.int32)
    earlier = jnp.cumsum(counts, axis=0) - counts
    rank = jnp.sum(earlier * counts, axis=1)
    picked = jnp.take(flat, active_rows, axis=0)
    contact = normalize(picked).astype(jnp.bfloat16)
    share = rank // per_sub
    slot = (share * n_exp + chosen) * per_sub + rank % per_sub
    placing = (
        jnp.arange(n_section * n_exp * per_sub, dtype=jnp.int32)[:, None] == slot[None, :]
    ).astype(jnp.bfloat16)
    dispatch = jnp.dot(placing, contact, preferred_element_type=jnp.float32).astype(jnp.bfloat16)
    dispatch = dispatch.reshape(n_section, n_exp * per_sub, width)
    columns = flat.reshape(rows_dev, n_section, part_width).transpose(1, 0, 2)
    columns = columns.reshape(n_section, rows_dev * part_width // width, width)
    payload = jnp.concatenate([columns, dispatch], axis=1)
    mine = payload[last]
    for target in range(n_section - 1):
        got = lax.ppermute(payload[target], "section", [(last, target)])
        mine = jnp.where(section == target, got, mine)
    base_rows = rows_dev * part_width // width
    base = mine[:base_rows].reshape(rows_dev, part_width)
    outgoing = mine[base_rows:].reshape(n_exp, per_sub, width)
    arrived = lax.all_to_all(outgoing, "expert", split_axis=0, concat_axis=0, tiled=True)
    rows = lax.all_gather(arrived, "section", axis=0, tiled=True).reshape(-1, width)
    e_first = exp_in[0]
    e_second = exp_out[0]
    column = lax.dynamic_slice_in_dim(router, expert_index, 1, 1)
    logits = jnp.dot(rows, column, preferred_element_type=jnp.float32)[:, 0]
    gate = jax.nn.sigmoid(logits)
    hidden = jax.nn.silu(jnp.dot(rows, e_first, preferred_element_type=jnp.float32)).astype(
        jnp.bfloat16
    )
    partial_value = jnp.dot(hidden, e_second, preferred_element_type=jnp.float32)
    scaled = (gate[:, None] * partial_value).astype(jnp.bfloat16)
    summed = lax.psum_scatter(scaled, "section", scatter_dimension=1, tiled=True)
    summed = summed.reshape(n_section, n_expert, per_sub, part_width).transpose(1, 0, 2, 3)
    returned = lax.all_to_all(summed, "expert", split_axis=0, concat_axis=0, tiled=True)
    returned = returned.reshape(n_exp * ranks, part_width)
    position = chosen * ranks + rank
    added = jnp.take(returned, position, axis=0).astype(jnp.float32)
    mixed = base.astype(jnp.float32).at[active_rows].add(added)
    return mixed.astype(jnp.bfloat16).reshape(micro, tok_dev, part_width)


def solution(mesh):
    return jax.shard_map(
        local,
        mesh=mesh,
        in_specs=(
            P(None, "expert", None),
            P("section", "expert", None),
            P("section", "expert", None),
            P(),
            P("expert", None, "section"),
            P("expert", "section", None),
            P("expert"),
            P("expert", None),
        ),
        out_specs=P(None, "expert", "section"),
        check_vma=False,
    )
```

profile of v0, /device:TPU:7, one launch (start us, length us, event | category | flops | bytes accessed | tf_op | source)
XLA Modules:
  0.0 662.8 jit_solution(12632711766562289976)
XLA Ops:
  12.4 97.6 %all-gather.4.cloned.1.call-done = bf16[1,2048,2048]{2,1,0:T(8,128)(2,1)} async-done(((bf16[1,64,2048]{2,1,0:T(8,128)(2,1)}), bf16[1,2048,2048]{2,1,0:T(8,128)(2,1)}) %all-gather.4.cloned.1.call-update) | async-done | bytes 8388624 | tf_op jit(solution)/shard_map/all_gather | solution.py:35
  110.0 97.6 %all-gather.6.cloned.1.call-done = bf16[1,2048,2048]{2,1,0:T(8,128)(2,1)} async-done(((bf16[1,64,2048]{2,1,0:T(8,128)(2,1)}), bf16[1,2048,2048]{2,1,0:T(8,128)(2,1)}) %all-gather.6.cloned.1.call-update) | async-done | bytes 8388624 | tf_op jit(solution)/shard_map/all_gather | solution.py:36
  208.6 290.4 %while.16 = (s32[]{:T(128)}, bf16[72,2048]{1,0:T(8,128)(2,1)}, bf16[8,72,2048]{2,1,0:T(8,128)(2,1)S(1)}, s32[]{:T(128)}, pred[]{:T(512)}, /*index=5*/bf16[8,72,2...) while((s32[]{:T(128)}, bf16[72,2048]{1,0:T(8,128)(2,1)}, ...), condition=%wide.region_4.5_spmd, body=%wide.region_0.4_spmd.sunk | while | flops 1210613888 | bytes 21499308 | solution.py:62
  211.5 3.3 collective-permute-done
  217.7 6.9 %collective-permute-done = bf16[72,2048]{1,0:T(8,128)(2,1)} collective-permute-done((bf16[72,2048]{1,0:T(8,128)(2,1)}, bf16[72,2048]{1,0:T(8,128)(2,1)}, u32[]{:S(2)}, u32[]{:S(2)}) %collective-permute-start) | collective-permute-done | bytes 294944 | tf_op jit(solution)/shard_map/while/body/eval_jaxpr/ppermute | solution.py:10
  224.6 1.5 conditional.2
  227.5 6.9 %collective-permute-done = bf16[72,2048]{1,0:T(8,128)(2,1)} collective-permute-done((bf16[72,2048]{1,0:T(8,128)(2,1)}, bf16[72,2048]{1,0:T(8,128)(2,1)}, u32[]{:S(2)}, u32[]{:S(2)}) %collective-permute-start) | collective-permute-done | bytes 294944 | tf_op jit(solution)/shard_map/while/body/eval_jaxpr/ppermute | solution.py:10
  237.4 6.9 %collective-permute-done = bf16[72,2048]{1,0:T(8,128)(2,1)} collective-permute-done((bf16[72,2048]{1,0:T(8,128)(2,1)}, bf16[72,2048]{1,0:T(8,128)(2,1)}, u32[]{:S(2)}, u32[]{:S(2)}) %collective-permute-start) | collective-permute-done | bytes 294944 | tf_op jit(solution)/shard_map/while/body/eval_jaxpr/ppermute | solution.py:10
  247.2 6.9 %collective-permute-done = bf16[72,2048]{1,0:T(8,128)(2,1)} collective-permute-done((bf16[72,2048]{1,0:T(8,128)(2,1)}, bf16[72,2048]{1,0:T(8,128)(2,1)}, u32[]{:S(2)}, u32[]{:S(2)}) %collective-permute-start) | collective-permute-done | bytes 294944 | tf_op jit(solution)/shard_map/while/body/eval_jaxpr/ppermute | solution.py:10
  257.0 6.9 %collective-permute-done = bf16[72,2048]{1,0:T(8,128)(2,1)} collective-permute-done((bf16[72,2048]{1,0:T(8,128)(2,1)}, bf16[72,2048]{1,0:T(8,128)(2,1)}, u32[]{:S(2)}, u32[]{:S(2)}) %collective-permute-start) | collective-permute-done | bytes 294944 | tf_op jit(solution)/shard_map/while/body/eval_jaxpr/ppermute | solution.py:10
  266.8 67.4 %collective-permute-done = bf16[72,2048]{1,0:T(8,128)(2,1)} collective-permute-done((bf16[72,2048]{1,0:T(8,128)(2,1)}, bf16[72,2048]{1,0:T(8,128)(2,1)}, u32[]{:S(2)}, u32[]{:S(2)}) %collective-permute-start) | collective-permute-done | bytes 294944 | tf_op jit(solution)/shard_map/while/body/eval_jaxpr/ppermute | solution.py:10
  334.3 12.8 %conditional.2 = (bf16[72,2048]{1,0:T(8,128)(2,1)}, bf16[1,72,2048]{2,1,0:T(8,128)(2,1)}) conditional(s32[]{:T(128)} %convert_element_type.108, () %tuple.53, (pred[]{:T(512)}, bf16[8,72,2048]{2,1,0:T(8,128)(2,1)}, s32[]{:T(128)}, bf16[72,2048]{1,0:T(8,128)(2,1)}, bf16[2048,2048]{1,0:T(8,128)(2,1)}, /*index=5*/bf16[2048,2048]{1,0:T(8,128)(2,1)}) %tuple.54), branch_computations={%region_1.1_spmd, %region_2.3_spmd} | conditional | flops 1210466432 | bytes 19434644 | solution.py:55
  335.6 9.8 %fusion = bf16[72,2048]{1,0:T(8,128)(2,1)} fusion(bf16[2048,2048]{1,0:T(8,128)(2,1)} %get-tuple-element.195, bf16[2048,2048]{1,0:T(8,128)(2,1)} %get-tuple-element.194, f32[72]{0:T(128)S(1)} %add_rsqrt_fusion, bf16[72,2048]{1,0:T(8,128)(2,1)} %get-tuple-element.193, bf16[8,72,2048]{2,1,0:T(8,128)(2,1)} %get-tuple-element.191, s32[]{:T(128)} %get-tuple-element.192, ...), kind=kOutput, calls=%fused_computation.4 | convolution fusion | flops 1209876480 | bytes 18254112 | tf_op jit(solution)/shard_map/while/body/eval_jaxpr/cond/branch_1_fun/dot_general | solution.py:24
  345.4 1.7 copy.30
  349.5 6.0 collective-permute-done
  355.4 12.8 %conditional.2 = (bf16[72,2048]{1,0:T(8,128)(2,1)}, bf16[1,72,2048]{2,1,0:T(8,128)(2,1)}) conditional(s32[]{:T(128)} %convert_element_type.108, () %tuple.53, (pred[]{:T(512)}, bf16[8,72,2048]{2,1,0:T(8,128)(2,1)}, s32[]{:T(128)}, bf16[72,2048]{1,0:T(8,128)(2,1)}, bf16[2048,2048]{1,0:T(8,128)(2,1)}, /*index=5*/bf16[2048,2048]{1,0:T(8,128)(2,1)}) %tuple.54), branch_computations={%region_1.1_spmd, %region_2.3_spmd} | conditional | flops 1210466432 | bytes 19434644 | solution.py:55
  356.7 9.8 %fusion = bf16[72,2048]{1,0:T(8,128)(2,1)} fusion(bf16[2048,2048]{1,0:T(8,128)(2,1)} %get-tuple-element.195, bf16[2048,2048]{1,0:T(8,128)(2,1)} %get-tuple-element.194, f32[72]{0:T(128)S(1)} %add_rsqrt_fusion, bf16[72,2048]{1,0:T(8,128)(2,1)} %get-tuple-element.193, bf16[8,72,2048]{2,1,0:T(8,128)(2,1)} %get-tuple-element.191, s32[]{:T(128)} %get-tuple-element.192, ...), kind=kOutput, calls=%fused_computation.4 | convolution fusion | flops 1209876480 | bytes 18254112 | tf_op jit(solution)/shard_map/while/body/eval_jaxpr/cond/branch_1_fun/dot_general | solution.py:24
  366.6 1.7 copy.30
  370.6 6.0 collective-permute-done
  376.6 12.8 %conditional.2 = (bf16[72,2048]{1,0:T(8,128)(2,1)}, bf16[1,72,2048]{2,1,0:T(8,128)(2,1)}) conditional(s32[]{:T(128)} %convert_element_type.108, () %tuple.53, (pred[]{:T(512)}, bf16[8,72,2048]{2,1,0:T(8,128)(2,1)}, s32[]{:T(128)}, bf16[72,2048]{1,0:T(8,128)(2,1)}, bf16[2048,2048]{1,0:T(8,128)(2,1)}, /*index=5*/bf16[2048,2048]{1,0:T(8,128)(2,1)}) %tuple.54), branch_computations={%region_1.1_spmd, %region_2.3_spmd} | conditional | flops 1210466432 | bytes 19434644 | solution.py:55
  377.9 9.8 %fusion = bf16[72,2048]{1,0:T(8,128)(2,1)} fusion(bf16[2048,2048]{1,0:T(8,128)(2,1)} %get-tuple-element.195, bf16[2048,2048]{1,0:T(8,128)(2,1)} %get-tuple-element.194, f32[72]{0:T(128)S(1)} %add_rsqrt_fusion, bf16[72,2048]{1,0:T(8,128)(2,1)} %get-tuple-element.193, bf16[8,72,2048]{2,1,0:T(8,128)(2,1)} %get-tuple-element.191, s32[]{:T(128)} %get-tuple-element.192, ...), kind=kOutput, calls=%fused_computation.4 | convolution fusion | flops 1209876480 | bytes 18254112 | tf_op jit(solution)/shard_map/while/body/eval_jaxpr/cond/branch_1_fun/dot_general | solution.py:24
  387.7 1.7 copy.30
  391.8 6.0 collective-permute-done
  397.8 12.8 %conditional.2 = (bf16[72,2048]{1,0:T(8,128)(2,1)}, bf16[1,72,2048]{2,1,0:T(8,128)(2,1)}) conditional(s32[]{:T(128)} %convert_element_type.108, () %tuple.53, (pred[]{:T(512)}, bf16[8,72,2048]{2,1,0:T(8,128)(2,1)}, s32[]{:T(128)}, bf16[72,2048]{1,0:T(8,128)(2,1)}, bf16[2048,2048]{1,0:T(8,128)(2,1)}, /*index=5*/bf16[2048,2048]{1,0:T(8,128)(2,1)}) %tuple.54), branch_computations={%region_1.1_spmd, %region_2.3_spmd} | conditional | flops 1210466432 | bytes 19434644 | solution.py:55
  399.0 9.8 %fusion = bf16[72,2048]{1,0:T(8,128)(2,1)} fusion(bf16[2048,2048]{1,0:T(8,128)(2,1)} %get-tuple-element.195, bf16[2048,2048]{1,0:T(8,128)(2,1)} %get-tuple-element.194, f32[72]{0:T(128)S(1)} %add_rsqrt_fusion, bf16[72,2048]{1,0:T(8,128)(2,1)} %get-tuple-element.193, bf16[8,72,2048]{2,1,0:T(8,128)(2,1)} %get-tuple-element.191, s32[]{:T(128)} %get-tuple-element.192, ...), kind=kOutput, calls=%fused_computation.4 | convolution fusion | flops 1209876480 | bytes 18254112 | tf_op jit(solution)/shard_map/while/body/eval_jaxpr/cond/branch_1_fun/dot_general | solution.py:24
  408.9 1.7 copy.30
  412.9 6.0 collective-permute-done
  418.9 12.8 %conditional.2 = (bf16[72,2048]{1,0:T(8,128)(2,1)}, bf16[1,72,2048]{2,1,0:T(8,128)(2,1)}) conditional(s32[]{:T(128)} %convert_element_type.108, () %tuple.53, (pred[]{:T(512)}, bf16[8,72,2048]{2,1,0:T(8,128)(2,1)}, s32[]{:T(128)}, bf16[72,2048]{1,0:T(8,128)(2,1)}, bf16[2048,2048]{1,0:T(8,128)(2,1)}, /*index=5*/bf16[2048,2048]{1,0:T(8,128)(2,1)}) %tuple.54), branch_computations={%region_1.1_spmd, %region_2.3_spmd} | conditional | flops 1210466432 | bytes 19434644 | solution.py:55
  420.2 9.8 %fusion = bf16[72,2048]{1,0:T(8,128)(2,1)} fusion(bf16[2048,2048]{1,0:T(8,128)(2,1)} %get-tuple-element.195, bf16[2048,2048]{1,0:T(8,128)(2,1)} %get-tuple-element.194, f32[72]{0:T(128)S(1)} %add_rsqrt_fusion, bf16[72,2048]{1,0:T(8,128)(2,1)} %get-tuple-element.193, bf16[8,72,2048]{2,1,0:T(8,128)(2,1)} %get-tuple-element.191, s32[]{:T(128)} %get-tuple-element.192, ...), kind=kOutput, calls=%fused_computation.4 | convolution fusion | flops 1209876480 | bytes 18254112 | tf_op jit(solution)/shard_map/while/body/eval_jaxpr/cond/branch_1_fun/dot_general | solution.py:24
  430.0 1.7 copy.30
  434.1 6.0 collective-permute-done
  440.1 12.8 %conditional.2 = (bf16[72,2048]{1,0:T(8,128)(2,1)}, bf16[1,72,2048]{2,1,0:T(8,128)(2,1)}) conditional(s32[]{:T(128)} %convert_element_type.108, () %tuple.53, (pred[]{:T(512)}, bf16[8,72,2048]{2,1,0:T(8,128)(2,1)}, s32[]{:T(128)}, bf16[72,2048]{1,0:T(8,128)(2,1)}, bf16[2048,2048]{1,0:T(8,128)(2,1)}, /*index=5*/bf16[2048,2048]{1,0:T(8,128)(2,1)}) %tuple.54), branch_computations={%region_1.1_spmd, %region_2.3_spmd} | conditional | flops 1210466432 | bytes 19434644 | solution.py:55
  441.3 9.8 %fusion = bf16[72,2048]{1,0:T(8,128)(2,1)} fusion(bf16[2048,2048]{1,0:T(8,128)(2,1)} %get-tuple-element.195, bf16[2048,2048]{1,0:T(8,128)(2,1)} %get-tuple-element.194, f32[72]{0:T(128)S(1)} %add_rsqrt_fusion, bf16[72,2048]{1,0:T(8,128)(2,1)} %get-tuple-element.193, bf16[8,72,2048]{2,1,0:T(8,128)(2,1)} %get-tuple-element.191, s32[]{:T(128)} %get-tuple-element.192, ...), kind=kOutput, calls=%fused_computation.4 | convolution fusion | flops 1209876480 | bytes 18254112 | tf_op jit(solution)/shard_map/while/body/eval_jaxpr/cond/branch_1_fun/dot_general | solution.py:24
  451.2 1.7 copy.30
  455.2 6.0 collective-permute-done
  461.2 12.8 %conditional.2 = (bf16[72,2048]{1,0:T(8,128)(2,1)}, bf16[1,72,2048]{2,1,0:T(8,128)(2,1)}) conditional(s32[]{:T(128)} %convert_element_type.108, () %tuple.53, (pred[]{:T(512)}, bf16[8,72,2048]{2,1,0:T(8,128)(2,1)}, s32[]{:T(128)}, bf16[72,2048]{1,0:T(8,128)(2,1)}, bf16[2048,2048]{1,0:T(8,128)(2,1)}, /*index=5*/bf16[2048,2048]{1,0:T(8,128)(2,1)}) %tuple.54), branch_computations={%region_1.1_spmd, %region_2.3_spmd} | conditional | flops 1210466432 | bytes 19434644 | solution.py:55
  462.5 9.8 %fusion = bf16[72,2048]{1,0:T(8,128)(2,1)} fusion(bf16[2048,2048]{1,0:T(8,128)(2,1)} %get-tuple-element.195, bf16[2048,2048]{1,0:T(8,128)(2,1)} %get-tuple-element.194, f32[72]{0:T(128)S(1)} %add_rsqrt_fusion, bf16[72,2048]{1,0:T(8,128)(2,1)} %get-tuple-element.193, bf16[8,72,2048]{2,1,0:T(8,128)(2,1)} %get-tuple-element.191, s32[]{:T(128)} %get-tuple-element.192, ...), kind=kOutput, calls=%fused_computation.4 | convolution fusion | flops 1209876480 | bytes 18254112 | tf_op jit(solution)/shard_map/while/body/eval_jaxpr/cond/branch_1_fun/dot_general | solution.py:24
  472.4 1.7 copy.30
  476.4 6.0 collective-permute-done
  482.4 12.8 %conditional.2 = (bf16[72,2048]{1,0:T(8,128)(2,1)}, bf16[1,72,2048]{2,1,0:T(8,128)(2,1)}) conditional(s32[]{:T(128)} %convert_element_type.108, () %tuple.53, (pred[]{:T(512)}, bf16[8,72,2048]{2,1,0:T(8,128)(2,1)}, s32[]{:T(128)}, bf16[72,2048]{1,0:T(8,128)(2,1)}, bf16[2048,2048]{1,0:T(8,128)(2,1)}, /*index=5*/bf16[2048,2048]{1,0:T(8,128)(2,1)}) %tuple.54), branch_computations={%region_1.1_spmd, %region_2.3_spmd} | conditional | flops 1210466432 | bytes 19434644 | solution.py:55
  483.7 9.8 %fusion = bf16[72,2048]{1,0:T(8,128)(2,1)} fusion(bf16[2048,2048]{1,0:T(8,128)(2,1)} %get-tuple-element.195, bf16[2048,2048]{1,0:T(8,128)(2,1)} %get-tuple-element.194, f32[72]{0:T(128)S(1)} %add_rsqrt_fusion, bf16[72,2048]{1,0:T(8,128)(2,1)} %get-tuple-element.193, bf16[8,72,2048]{2,1,0:T(8,128)(2,1)} %get-tuple-element.191, s32[]{:T(128)} %get-tuple-element.192, ...), kind=kOutput, calls=%fused_computation.4 | convolution fusion | flops 1209876480 | bytes 18254112 | tf_op jit(solution)/shard_map/while/body/eval_jaxpr/cond/branch_1_fun/dot_general | solution.py:24
  493.5 1.7 copy.30
  499.0 1.8 gather_fusion
  503.0 1.9 copy.25
  504.9 3.7 reshape.112
  508.6 1.9 convolution_convert_fusion
  510.5 1.7 fusion.43
  512.7 2.1 collective-permute-start.1
  516.1 2.1 collective-permute-start.3
  518.2 2.1 collective-permute-start.4
  520.3 2.1 collective-permute-start.5
  522.4 2.1 collective-permute-start.6
  525.3 2.1 collective-permute-start.7
  528.6 6.0 collective-permute-done.4
  534.6 6.0 collective-permute-done.5
  540.6 1.7 fusion.36
  543.3 15.7 %all_to_all.10 = bf16[32,2,2048]{2,1,0:T(2,128)(2,1)} all-to-all(bf16[32,2,2048]{2,1,0:T(2,128)(2,1)S(1)} %reshape.117), channel_id=1, replica_groups=mesh['section'=8,'expert'=32] {'expert'}, dimensions={0} | all-to-all | bytes 524288 | tf_op jit(solution)/shard_map/all_to_all | solution.py:93
  559.2 24.6 %all-gather.8.cloned.1.call-done = bf16[256,2,2048]{2,1,0:T(2,128)(2,1)} async-done(((bf16[32,2,2048]{2,1,0:T(2,128)(2,1)}), bf16[256,2,2048]{2,1,0:T(2,128)(2,1)}) %all-gather.8.cloned.1.call-update) | async-done | bytes 2097168 | tf_op jit(solution)/shard_map/all_gather | solution.py:94
  583.8 2.7 reshape.118
  588.0 4.9 multiply_convert_fusion.2
  593.0 36.3 %reduce-scatter.2.cloned.1.call-done = bf16[512,256]{1,0:T(8,128)(2,1)} async-done(((bf16[512,2048]{1,0:T(8,128)(2,1)}), bf16[512,256]{1,0:T(8,128)(2,1)}) %reduce-scatter.2.cloned.1.call-update) | async-done | bytes 262160 | tf_op jit(solution)/shard_map/reduce_scatter | solution.py:105
  631.2 9.3 %all-to-all-start.1 = ((bf16[32,8,2,256]{3,2,1,0:T(2,128)(2,1)}), bf16[32,8,2,256]{3,2,1,0:T(2,128)(2,1)S(1)}, u32[]{:S(2)}, u32[]{:S(2)}) async-start(bf16[32,8,2,256]{3,2,1,0:T(2,128)(2,1)} %bitcast.85), calls=%async_computation.2 | async-start | bytes 524288 | tf_op jit(solution)/shard_map/all_to_all | solution.py:107
  640.7 12.6 %all-to-all-done.1 = bf16[32,8,2,256]{3,2,1,0:T(2,128)(2,1)S(1)} async-done(((bf16[32,8,2,256]{3,2,1,0:T(2,128)(2,1)}), bf16[32,8,2,256]{3,2,1,0:T(2,128)(2,1)S(1)}, u32[]{:S(2)}, u32[]{:S(2)}) %all-to-all-start.1) | async-done | bytes 262176 | tf_op jit(solution)/shard_map/all_to_all | solution.py:107
  653.4 2.1 scatter_custom_fusion
  (124 shorter events, 77.6 us)
Async XLA Ops:
  6.5 581.4 %copy-start = (bf16[1,256,2048]{2,1,0:T(8,128)(2,1)S(1)}, bf16[1,256,2048]{2,1,0:T(8,128)(2,1)}, u32[]{:S(2)}) copy-start(bf16[1,256,2048]{2,1,0:T(8,128)(2,1)} %param.17) | copy-start | bytes 3145732
  6.5 103.5 %all-gather.4.cloned.1.call-start = ((), (), s32[]{:S(2)}) async-start(), calls=%async_computation.3 | async-start | bytes 8650752 | tf_op jit(solution)/shard_map/all_gather | solution.py:35
  7.3 200.3 %all-gather.6.cloned.1.call-start = ((), (), s32[]{:S(2)}) async-start(), calls=%async_computation.4 | async-start | bytes 8650752 | tf_op jit(solution)/shard_map/all_gather | solution.py:36
  8.0 575.8 %all-gather.8.cloned.1.call-start = ((), (), s32[]{:S(2)}) async-start(), calls=%async_computation.5 | async-start | bytes 2359296 | tf_op jit(solution)/shard_map/all_gather | solution.py:94
  210.1 4.7 collective-permute-start
  216.3 8.3 %collective-permute-start = (bf16[72,2048]{1,0:T(8,128)(2,1)}, bf16[72,2048]{1,0:T(8,128)(2,1)}, u32[]{:S(2)}, u32[]{:S(2)}) collective-permute-start(bf16[72,2048]{1,0:T(8,128)(2,1)} %get-tuple-element.294), channel_id=1, source_target_pairs={{0,32},{32,64},{64,96},{96,128},{128,160},{160,192},{192,224},{1,3... | collective-permute-start | bytes 884744 | tf_op jit(solution)/shard_map/while/body/eval_jaxpr/ppermute | solution.py:10
  226.1 8.3 %collective-permute-start = (bf16[72,2048]{1,0:T(8,128)(2,1)}, bf16[72,2048]{1,0:T(8,128)(2,1)}, u32[]{:S(2)}, u32[]{:S(2)}) collective-permute-start(bf16[72,2048]{1,0:T(8,128)(2,1)} %get-tuple-element.294), channel_id=1, source_target_pairs={{0,32},{32,64},{64,96},{96,128},{128,160},{160,192},{192,224},{1,3... | collective-permute-start | bytes 884744 | tf_op jit(solution)/shard_map/while/body/eval_jaxpr/ppermute | solution.py:10
  236.0 8.3 %collective-permute-start = (bf16[72,2048]{1,0:T(8,128)(2,1)}, bf16[72,2048]{1,0:T(8,128)(2,1)}, u32[]{:S(2)}, u32[]{:S(2)}) collective-permute-start(bf16[72,2048]{1,0:T(8,128)(2,1)} %get-tuple-element.294), channel_id=1, source_target_pairs={{0,32},{32,64},{64,96},{96,128},{128,160},{160,192},{192,224},{1,3... | collective-permute-start | bytes 884744 | tf_op jit(solution)/shard_map/while/body/eval_jaxpr/ppermute | solution.py:10
  245.8 8.3 %collective-permute-start = (bf16[72,2048]{1,0:T(8,128)(2,1)}, bf16[72,2048]{1,0:T(8,128)(2,1)}, u32[]{:S(2)}, u32[]{:S(2)}) collective-permute-start(bf16[72,2048]{1,0:T(8,128)(2,1)} %get-tuple-element.294), channel_id=1, source_target_pairs={{0,32},{32,64},{64,96},{96,128},{128,160},{160,192},{192,224},{1,3... | collective-permute-start | bytes 884744 | tf_op jit(solution)/shard_map/while/body/eval_jaxpr/ppermute | solution.py:10
  255.6 8.3 %collective-permute-start = (bf16[72,2048]{1,0:T(8,128)(2,1)}, bf16[72,2048]{1,0:T(8,128)(2,1)}, u32[]{:S(2)}, u32[]{:S(2)}) collective-permute-start(bf16[72,2048]{1,0:T(8,128)(2,1)} %get-tuple-element.294), channel_id=1, source_target_pairs={{0,32},{32,64},{64,96},{96,128},{128,160},{160,192},{192,224},{1,3... | collective-permute-start | bytes 884744 | tf_op jit(solution)/shard_map/while/body/eval_jaxpr/ppermute | solution.py:10
  265.4 68.8 %collective-permute-start = (bf16[72,2048]{1,0:T(8,128)(2,1)}, bf16[72,2048]{1,0:T(8,128)(2,1)}, u32[]{:S(2)}, u32[]{:S(2)}) collective-permute-start(bf16[72,2048]{1,0:T(8,128)(2,1)} %get-tuple-element.294), channel_id=1, source_target_pairs={{0,32},{32,64},{64,96},{96,128},{128,160},{160,192},{192,224},{1,3... | collective-permute-start | bytes 884744 | tf_op jit(solution)/shard_map/while/body/eval_jaxpr/ppermute | solution.py:10
  347.1 8.4 %collective-permute-start = (bf16[72,2048]{1,0:T(8,128)(2,1)}, bf16[72,2048]{1,0:T(8,128)(2,1)}, u32[]{:S(2)}, u32[]{:S(2)}) collective-permute-start(bf16[72,2048]{1,0:T(8,128)(2,1)} %get-tuple-element.294), channel_id=1, source_target_pairs={{0,32},{32,64},{64,96},{96,128},{128,160},{160,192},{192,224},{1,3... | collective-permute-start | bytes 884744 | tf_op jit(solution)/shard_map/while/body/eval_jaxpr/ppermute | solution.py:10
  368.3 8.3 %collective-permute-start = (bf16[72,2048]{1,0:T(8,128)(2,1)}, bf16[72,2048]{1,0:T(8,128)(2,1)}, u32[]{:S(2)}, u32[]{:S(2)}) collective-permute-start(bf16[72,2048]{1,0:T(8,128)(2,1)} %get-tuple-element.294), channel_id=1, source_target_pairs={{0,32},{32,64},{64,96},{96,128},{128,160},{160,192},{192,224},{1,3... | collective-permute-start | bytes 884744 | tf_op jit(solution)/shard_map/while/body/eval_jaxpr/ppermute | solution.py:10
  389.4 8.3 %collective-permute-start = (bf16[72,2048]{1,0:T(8,128)(2,1)}, bf16[72,2048]{1,0:T(8,128)(2,1)}, u32[]{:S(2)}, u32[]{:S(2)}) collective-permute-start(bf16[72,2048]{1,0:T(8,128)(2,1)} %get-tuple-element.294), channel_id=1, source_target_pairs={{0,32},{32,64},{64,96},{96,128},{128,160},{160,192},{192,224},{1,3... | collective-permute-start | bytes 884744 | tf_op jit(solution)/shard_map/while/body/eval_jaxpr/ppermute | solution.py:10
  410.6 8.3 %collective-permute-start = (bf16[72,2048]{1,0:T(8,128)(2,1)}, bf16[72,2048]{1,0:T(8,128)(2,1)}, u32[]{:S(2)}, u32[]{:S(2)}) collective-permute-start(bf16[72,2048]{1,0:T(8,128)(2,1)} %get-tuple-element.294), channel_id=1, source_target_pairs={{0,32},{32,64},{64,96},{96,128},{128,160},{160,192},{192,224},{1,3... | collective-permute-start | bytes 884744 | tf_op jit(solution)/shard_map/while/body/eval_jaxpr/ppermute | solution.py:10
  431.7 8.3 %collective-permute-start = (bf16[72,2048]{1,0:T(8,128)(2,1)}, bf16[72,2048]{1,0:T(8,128)(2,1)}, u32[]{:S(2)}, u32[]{:S(2)}) collective-permute-start(bf16[72,2048]{1,0:T(8,128)(2,1)} %get-tuple-element.294), channel_id=1, source_target_pairs={{0,32},{32,64},{64,96},{96,128},{128,160},{160,192},{192,224},{1,3... | collective-permute-start | bytes 884744 | tf_op jit(solution)/shard_map/while/body/eval_jaxpr/ppermute | solution.py:10
  452.9 8.3 %collective-permute-start = (bf16[72,2048]{1,0:T(8,128)(2,1)}, bf16[72,2048]{1,0:T(8,128)(2,1)}, u32[]{:S(2)}, u32[]{:S(2)}) collective-permute-start(bf16[72,2048]{1,0:T(8,128)(2,1)} %get-tuple-element.294), channel_id=1, source_target_pairs={{0,32},{32,64},{64,96},{96,128},{128,160},{160,192},{192,224},{1,3... | collective-permute-start | bytes 884744 | tf_op jit(solution)/shard_map/while/body/eval_jaxpr/ppermute | solution.py:10
  474.0 8.3 %collective-permute-start = (bf16[72,2048]{1,0:T(8,128)(2,1)}, bf16[72,2048]{1,0:T(8,128)(2,1)}, u32[]{:S(2)}, u32[]{:S(2)}) collective-permute-start(bf16[72,2048]{1,0:T(8,128)(2,1)} %get-tuple-element.294), channel_id=1, source_target_pairs={{0,32},{32,64},{64,96},{96,128},{128,160},{160,192},{192,224},{1,3... | collective-permute-start | bytes 884744 | tf_op jit(solution)/shard_map/while/body/eval_jaxpr/ppermute | solution.py:10
  495.2 3.8 collective-permute-start
  510.4 2.3 copy-start.1
  512.7 9.7 %collective-permute-start.1 = (bf16[136,2048]{1,0:T(8,128)(2,1)S(1)}, bf16[136,2048]{1,0:T(8,128)(2,1)S(1)}, u32[]{:S(2)}, u32[]{:S(2)}) collective-permute-start(bf16[136,2048]{1,0:T(8,128)(2,1)S(1)} %get-tuple-element.231), channel_id=1, source_target_pairs={{224,192},{225,193},{226,194},{227,195},{228,196},{229,197},{230,1... | collective-permute-start | bytes 1671176 | tf_op jit(solution)/shard_map/ppermute | solution.py:88
  514.8 9.7 %collective-permute-start.2 = (bf16[136,2048]{1,0:T(8,128)(2,1)S(1)}, bf16[136,2048]{1,0:T(8,128)(2,1)S(1)}, u32[]{:S(2)}, u32[]{:S(2)}) collective-permute-start(bf16[136,2048]{1,0:T(8,128)(2,1)S(1)} %get-tuple-element.232), channel_id=1, source_target_pairs={{224,160},{225,161},{226,162},{227,163},{228,164},{229,165},{230,1... | collective-permute-start | bytes 1671176 | tf_op jit(solution)/shard_map/ppermute | solution.py:88
  516.1 12.5 %collective-permute-start.3 = (bf16[136,2048]{1,0:T(8,128)(2,1)}, bf16[136,2048]{1,0:T(8,128)(2,1)}, u32[]{:S(2)}, u32[]{:S(2)}) collective-permute-start(bf16[136,2048]{1,0:T(8,128)(2,1)} %get-tuple-element.233), channel_id=1, source_target_pairs={{224,128},{225,129},{226,130},{227,131},{228,132},{229,133},{230,1... | collective-permute-start | bytes 1671176 | tf_op jit(solution)/shard_map/ppermute | solution.py:88
  518.2 16.3 %collective-permute-start.4 = (bf16[136,2048]{1,0:T(8,128)(2,1)}, bf16[136,2048]{1,0:T(8,128)(2,1)}, u32[]{:S(2)}, u32[]{:S(2)}) collective-permute-start(bf16[136,2048]{1,0:T(8,128)(2,1)} %get-tuple-element.234), channel_id=1, source_target_pairs={{224,96},{225,97},{226,98},{227,99},{228,100},{229,101},{230,102},... | collective-permute-start | bytes 1671176 | tf_op jit(solution)/shard_map/ppermute | solution.py:88
  520.3 20.2 %collective-permute-start.5 = (bf16[136,2048]{1,0:T(8,128)(2,1)}, bf16[136,2048]{1,0:T(8,128)(2,1)}, u32[]{:S(2)}, u32[]{:S(2)}) collective-permute-start(bf16[136,2048]{1,0:T(8,128)(2,1)} %get-tuple-element.235), channel_id=1, source_target_pairs={{224,64},{225,65},{226,66},{227,67},{228,68},{229,69},{230,70},{23... | collective-permute-start | bytes 1671176 | tf_op jit(solution)/shard_map/ppermute | solution.py:88
  522.4 2.1 copy-start.4
  522.4 18.1 %collective-permute-start.6 = (bf16[136,2048]{1,0:T(8,128)(2,1)}, bf16[136,2048]{1,0:T(8,128)(2,1)}, u32[]{:S(2)}, u32[]{:S(2)}) collective-permute-start(bf16[136,2048]{1,0:T(8,128)(2,1)} %get-tuple-element.236), channel_id=1, source_target_pairs={{224,32},{225,33},{226,34},{227,35},{228,36},{229,37},{230,38},{23... | collective-permute-start | bytes 1671176 | tf_op jit(solution)/shard_map/ppermute | solution.py:88
  524.5 0.8 copy-start.5
  525.3 15.2 %collective-permute-start.7 = (bf16[136,2048]{1,0:T(8,128)(2,1)}, bf16[136,2048]{1,0:T(8,128)(2,1)}, u32[]{:S(2)}, u32[]{:S(2)}) collective-permute-start(bf16[136,2048]{1,0:T(8,128)(2,1)} %get-tuple-element.230), channel_id=1, source_target_pairs={{224,0},{225,1},{226,2},{227,3},{228,4},{229,5},{230,6},{231,7},{2... | collective-permute-start | bytes 1671176 | tf_op jit(solution)/shard_map/ppermute | solution.py:88
  542.3 0.8 copy-start.2
  559.0 70.3 %reduce-scatter.2.cloned.1.call-start = ((), (), s32[]{:S(2)}) async-start(), calls=%async_computation.6 | async-start | bytes 2359296 | tf_op jit(solution)/shard_map/reduce_scatter | solution.py:105
  588.0 4.9 copy-start.6
  592.9 47.7 %copy-start.3 = (bf16[136,2048]{1,0:T(8,128)(2,1)S(1)}, bf16[136,2048]{1,0:T(8,128)(2,1)}, u32[]{:S(2)}) copy-start(bf16[136,2048]{1,0:T(8,128)(2,1)} %copy-done.2) | copy-start | bytes 1671172
  631.2 22.1 %all-to-all-start.1 = ((bf16[32,8,2,256]{3,2,1,0:T(2,128)(2,1)}), bf16[32,8,2,256]{3,2,1,0:T(2,128)(2,1)S(1)}, u32[]{:S(2)}, u32[]{:S(2)}) async-start(bf16[32,8,2,256]{3,2,1,0:T(2,128)(2,1)} %bitcast.85), calls=%async_computation.2 | async-start | bytes 524288 | tf_op jit(solution)/shard_map/all_to_all | solution.py:107
Sparse Core Ops, SparseCore 0:
  9.9 100.0 all-gather.3
  112.6 94.9 all-gather.5
  559.1 24.6 all-gather.7
  593.0 36.1 reduce-scatter.1
where the time goes:
time: 665 us; the launch traced here: 663 us
  waiting for transfers between devices  432 us (65%)
  matrix products  87 us (13%)
  starting transfers between devices  42.7 us (6%)
  local copies, waits for them, and re-layouts  40.5 us (6%)
  other arithmetic  31.2 us (5%)
  blocking collectives  15.7 us (2%)
  between operations  13.3 us (2%)
    ppermute x15, waiting for transfers between devices, from_behind(): lax.ppermute(value, axis, [(source, source + steps) for source in range(i...  149 us
    all_gather x1, waiting for transfers between devices, local(): lax.all_gather(w_out, 'expert', axis=1, tiled=True)  97.6 us
    all_gather x1, waiting for transfers between devices, local(): lax.all_gather(w_in, 'expert', axis=1, tiled=True)  97.6 us
    dot_general x8, matrix products, processor(): branch = jnp.dot(hidden, w_second, preferred_element_type=jnp.float32)  78.8 us
    reduce_scatter x1, waiting for transfers between devices, local(): lax.psum_scatter(scaled, 'section', scatter_dimension=1, tiled=True)  36.3 us
    all_gather x1, waiting for transfers between devices, local(): lax.all_gather(arrived, 'section', axis=0, tiled=True).reshape(-1, width)  24.6 us
    ppermute x15, starting transfers between devices, from_behind(): lax.ppermute(value, axis, [(source, source + steps) for source in range(i...  19.2 us
    all_to_all x1, blocking collectives, local(): lax.all_to_all(outgoing, 'expert', split_axis=0, concat_axis=0, tiled=True)  15.7 us
  transfers between devices with their start and end apart: 27, of which 23 were waited for; matrix products, arithmetic and copies ran while one was open for 2% of the time, Pallas kernels for 0%

commit v1 on v0

--- a/solution.py
+++ b/solution.py
@@ -1,7 +1,18 @@
+import functools
 import jax
 import jax.numpy as jnp
 from jax import lax
 from jax.sharding import PartitionSpec as P
+
+
+def enter_field(field, axis_key):
+    arr_out = tuple((field for _ in range(jax.lax.axis_size(axis_key))))
+    opened = jnp.stack(arr_out)
+    taken_in = jax.lax.all_to_all(opened, axis_name=axis_key, split_axis=0, concat_axis=0)
+    return jnp.concatenate(taken_in, axis=1)
+
+
+measure_knots = functools.partial(enter_field, axis_key="expert")
 
 
 def from_behind(value, axis, steps):
@@ -31,10 +42,7 @@
     section = lax.axis_index("section")
     expert_index = lax.axis_index("expert")
     micro, tok_dev, width = tokens.shape
-    w_first, w_second = (
-        lax.all_gather(w_in, "expert", axis=1, tiled=True),
-        lax.all_gather(w_out, "expert", axis=1, tiled=True),
-    )
+    w_first, w_second = (lax.all_gather(w_in, "expert", axis=1, tiled=True), measure_knots(w_out))
     w_first = w_first[0]
     w_second = w_second[0]
     last = n_section - 1

time: 665 us -> 717 us (1.078)
  waiting for transfers between devices: 432 us -> 466 us
  starting transfers between devices: 42.7 us -> 54.2 us
    all_to_all x0 -> x1, waiting for transfers between devices: none -> 229 us  [enter_field(): jax.lax.all_to_all(opened, axis_name=axis_key, split_axis=0, concat_axis=0)]
    all_gather x1 -> x0, waiting for transfers between devices: 97.6 us -> none  [local(): lax.all_gather(w_out, 'expert', axis=1, tiled=True)]
    all_gather x1, waiting for transfers between devices: 97.6 us -> 0.01 us  [local(): lax.all_gather(w_in, 'expert', axis=1, tiled=True)]
    all_to_all x0 -> x1, starting transfers between devices: none -> 11.5 us  [enter_field(): jax.lax.all_to_all(opened, axis_name=axis_key, split_axis=0, concat_axis=0)]
  transfers between devices with their start and end apart: 27 -> 27, of which waited for: 23 -> 22; matrix products, arithmetic and copies ran while one was open for 2% -> 1% of each run, Pallas kernels for 0% -> 0%
where the time goes in v1:
time: 717 us; the launch traced here: 715 us
  waiting for transfers between devices  466 us (65%)
  matrix products  87 us (12%)
  starting transfers between devices  54.2 us (8%)
  local copies, waits for them, and re-layouts  45.8 us (6%)
  other arithmetic  27.7 us (4%)
  blocking collectives  20.7 us (3%)
  between operations  13.4 us (2%)
    all_to_all x1, waiting for transfers between devices, enter_field(): jax.lax.all_to_all(opened, axis_name=axis_key, split_axis=0, concat_axis=0)  229 us
    ppermute x15, waiting for transfers between devices, from_behind(): lax.ppermute(value, axis, [(source, source + steps) for source in range(i...  149 us
    dot_general x8, matrix products, processor(): branch = jnp.dot(hidden, w_second, preferred_element_type=jnp.float32)  78.8 us
    reduce_scatter x1, waiting for transfers between devices, local(): lax.psum_scatter(scaled, 'section', scatter_dimension=1, tiled=True)  36.3 us
    all_gather x1, waiting for transfers between devices, local(): lax.all_gather(arrived, 'section', axis=0, tiled=True).reshape(-1, width)  24.6 us
    all_to_all x1, blocking collectives, local(): lax.all_to_all(outgoing, 'expert', split_axis=0, concat_axis=0, tiled=True)  20.7 us
    ppermute x15, starting transfers between devices, from_behind(): lax.ppermute(value, axis, [(source, source + steps) for source in range(i...  19.2 us
  transfers between devices with their start and end apart: 27, of which 22 were waited for; matrix products, arithmetic and copies ran while one was open for 1% of the time, Pallas kernels for 0%

profile of v1, /device:TPU:7, one launch (start us, length us, event | category | flops | bytes accessed | tf_op | source)
XLA Modules:
  0.0 715.0 jit_solution(4653836272457592735)
XLA Ops:
  6.5 5.3 stack.2
  11.9 11.5 %all-to-all-start = ((bf16[32,1,64,2048]{3,2,1,0:T(8,128)(2,1)}), bf16[32,1,64,2048]{3,2,1,0:T(8,128)(2,1)}, u32[]{:S(2)}, u32[]{:S(2)}) async-start(bf16[32,1,64,2048]{3,2,1,0:T(8,128)(2,1)} %stack.2), calls=%async_computation | async-start | bytes 16777216 | tf_op jit(solution)/shard_map/all_to_all | solution.py:11
  25.2 229.0 %all-to-all-done = bf16[32,1,64,2048]{3,2,1,0:T(8,128)(2,1)} async-done(((bf16[32,1,64,2048]{3,2,1,0:T(8,128)(2,1)}), bf16[32,1,64,2048]{3,2,1,0:T(8,128)(2,1)}, u32[]{:S(2)}, u32[]{:S(2)}) %all-to-all-start) | async-done | bytes 8388640 | tf_op jit(solution)/shard_map/all_to_all | solution.py:11
  255.2 291.0 %while.16 = (s32[]{:T(128)}, bf16[72,2048]{1,0:T(8,128)(2,1)}, bf16[8,72,2048]{2,1,0:T(8,128)(2,1)S(1)}, s32[]{:T(128)}, pred[]{:T(512)}, /*index=5*/bf16[8,72,2...) while((s32[]{:T(128)}, bf16[72,2048]{1,0:T(8,128)(2,1)}, ...), condition=%wide.region_4.5_spmd, body=%wide.region_0.4_spmd.sunk | while | flops 1210613888 | bytes 21499308 | solution.py:70
  258.1 4.0 collective-permute-done
  265.0 6.9 collective-permute-done
  274.8 6.9 collective-permute-done
  284.6 6.9 collective-permute-done
  294.5 6.9 collective-permute-done
  304.3 6.9 collective-permute-done
  314.1 67.4 %collective-permute-done = bf16[72,2048]{1,0:T(8,128)(2,1)} collective-permute-done((bf16[72,2048]{1,0:T(8,128)(2,1)}, bf16[72,2048]{1,0:T(8,128)(2,1)}, u32[]{:S(2)}, u32[]{:S(2)}) %collective-permute-start) | collective-permute-done | bytes 294944 | tf_op jit(solution)/shard_map/while/body/eval_jaxpr/ppermute | solution.py:21
  381.5 12.8 %conditional.2 = (bf16[72,2048]{1,0:T(8,128)(2,1)}, bf16[1,72,2048]{2,1,0:T(8,128)(2,1)}) conditional(s32[]{:T(128)} %convert_element_type.108, () %tuple.53, (pred[]{:T(512)}, bf16[8,72,2048]{2,1,0:T(8,128)(2,1)}, s32[]{:T(128)}, bf16[72,2048]{1,0:T(8,128)(2,1)}, bf16[2048,2048]{1,0:T(8,128)(2,1)}, /*index=5*/bf16[2048,2048]{1,0:T(8,128)(2,1)}) %tuple.54), branch_computations={%region_1.1_spmd, %region_2.3_spmd} | conditional | flops 1210466432 | bytes 19434644 | solution.py:63
  382.8 9.8 %fusion = bf16[72,2048]{1,0:T(8,128)(2,1)} fusion(bf16[2048,2048]{1,0:T(8,128)(2,1)} %get-tuple-element.195, bf16[2048,2048]{1,0:T(8,128)(2,1)} %get-tuple-element.194, f32[72]{0:T(128)S(1)} %add_rsqrt_fusion, bf16[72,2048]{1,0:T(8,128)(2,1)} %get-tuple-element.193, bf16[8,72,2048]{2,1,0:T(8,128)(2,1)} %get-tuple-element.191, s32[]{:T(128)} %get-tuple-element.192, ...), kind=kOutput, calls=%fused_computation.4 | convolution fusion | flops 1209876480 | bytes 18254112 | tf_op jit(solution)/shard_map/while/body/eval_jaxpr/cond/branch_1_fun/dot_general | solution.py:35
  392.6 1.7 copy.30
  396.7 6.0 collective-permute-done
  402.7 12.8 %conditional.2 = (bf16[72,2048]{1,0:T(8,128)(2,1)}, bf16[1,72,2048]{2,1,0:T(8,128)(2,1)}) conditional(s32[]{:T(128)} %convert_element_type.108, () %tuple.53, (pred[]{:T(512)}, bf16[8,72,2048]{2,1,0:T(8,128)(2,1)}, s32[]{:T(128)}, bf16[72,2048]{1,0:T(8,128)(2,1)}, bf16[2048,2048]{1,0:T(8,128)(2,1)}, /*index=5*/bf16[2048,2048]{1,0:T(8,128)(2,1)}) %tuple.54), branch_computations={%region_1.1_spmd, %region_2.3_spmd} | conditional | flops 1210466432 | bytes 19434644 | solution.py:63
  403.9 9.8 %fusion = bf16[72,2048]{1,0:T(8,128)(2,1)} fusion(bf16[2048,2048]{1,0:T(8,128)(2,1)} %get-tuple-element.195, bf16[2048,2048]{1,0:T(8,128)(2,1)} %get-tuple-element.194, f32[72]{0:T(128)S(1)} %add_rsqrt_fusion, bf16[72,2048]{1,0:T(8,128)(2,1)} %get-tuple-element.193, bf16[8,72,2048]{2,1,0:T(8,128)(2,1)} %get-tuple-element.191, s32[]{:T(128)} %get-tuple-element.192, ...), kind=kOutput, calls=%fused_computation.4 | convolution fusion | flops 1209876480 | bytes 18254112 | tf_op jit(solution)/shard_map/while/body/eval_jaxpr/cond/branch_1_fun/dot_general | solution.py:35
  413.8 1.7 copy.30
  417.8 6.0 collective-permute-done
  423.8 12.8 %conditional.2 = (bf16[72,2048]{1,0:T(8,128)(2,1)}, bf16[1,72,2048]{2,1,0:T(8,128)(2,1)}) conditional(s32[]{:T(128)} %convert_element_type.108, () %tuple.53, (pred[]{:T(512)}, bf16[8,72,2048]{2,1,0:T(8,128)(2,1)}, s32[]{:T(128)}, bf16[72,2048]{1,0:T(8,128)(2,1)}, bf16[2048,2048]{1,0:T(8,128)(2,1)}, /*index=5*/bf16[2048,2048]{1,0:T(8,128)(2,1)}) %tuple.54), branch_computations={%region_1.1_spmd, %region_2.3_spmd} | conditional | flops 1210466432 | bytes 19434644 | solution.py:63
  425.1 9.8 %fusion = bf16[72,2048]{1,0:T(8,128)(2,1)} fusion(bf16[2048,2048]{1,0:T(8,128)(2,1)} %get-tuple-element.195, bf16[2048,2048]{1,0:T(8,128)(2,1)} %get-tuple-element.194, f32[72]{0:T(128)S(1)} %add_rsqrt_fusion, bf16[72,2048]{1,0:T(8,128)(2,1)} %get-tuple-element.193, bf16[8,72,2048]{2,1,0:T(8,128)(2,1)} %get-tuple-element.191, s32[]{:T(128)} %get-tuple-element.192, ...), kind=kOutput, calls=%fused_computation.4 | convolution fusion | flops 1209876480 | bytes 18254112 | tf_op jit(solution)/shard_map/while/body/eval_jaxpr/cond/branch_1_fun/dot_general | solution.py:35
  434.9 1.7 copy.30
  439.0 6.0 collective-permute-done
  445.0 12.8 %conditional.2 = (bf16[72,2048]{1,0:T(8,128)(2,1)}, bf16[1,72,2048]{2,1,0:T(8,128)(2,1)}) conditional(s32[]{:T(128)} %convert_element_type.108, () %tuple.53, (pred[]{:T(512)}, bf16[8,72,2048]{2,1,0:T(8,128)(2,1)}, s32[]{:T(128)}, bf16[72,2048]{1,0:T(8,128)(2,1)}, bf16[2048,2048]{1,0:T(8,128)(2,1)}, /*index=5*/bf16[2048,2048]{1,0:T(8,128)(2,1)}) %tuple.54), branch_computations={%region_1.1_spmd, %region_2.3_spmd} | conditional | flops 1210466432 | bytes 19434644 | solution.py:63
  446.2 9.8 %fusion = bf16[72,2048]{1,0:T(8,128)(2,1)} fusion(bf16[2048,2048]{1,0:T(8,128)(2,1)} %get-tuple-element.195, bf16[2048,2048]{1,0:T(8,128)(2,1)} %get-tuple-element.194, f32[72]{0:T(128)S(1)} %add_rsqrt_fusion, bf16[72,2048]{1,0:T(8,128)(2,1)} %get-tuple-element.193, bf16[8,72,2048]{2,1,0:T(8,128)(2,1)} %get-tuple-element.191, s32[]{:T(128)} %get-tuple-element.192, ...), kind=kOutput, calls=%fused_computation.4 | convolution fusion | flops 1209876480 | bytes 18254112 | tf_op jit(solution)/shard_map/while/body/eval_jaxpr/cond/branch_1_fun/dot_general | solution.py:35
  456.1 1.7 copy.30
  460.1 6.0 collective-permute-done
  466.1 12.8 %conditional.2 = (bf16[72,2048]{1,0:T(8,128)(2,1)}, bf16[1,72,2048]{2,1,0:T(8,128)(2,1)}) conditional(s32[]{:T(128)} %convert_element_type.108, () %tuple.53, (pred[]{:T(512)}, bf16[8,72,2048]{2,1,0:T(8,128)(2,1)}, s32[]{:T(128)}, bf16[72,2048]{1,0:T(8,128)(2,1)}, bf16[2048,2048]{1,0:T(8,128)(2,1)}, /*index=5*/bf16[2048,2048]{1,0:T(8,128)(2,1)}) %tuple.54), branch_computations={%region_1.1_spmd, %region_2.3_spmd} | conditional | flops 1210466432 | bytes 19434644 | solution.py:63
  467.4 9.8 %fusion = bf16[72,2048]{1,0:T(8,128)(2,1)} fusion(bf16[2048,2048]{1,0:T(8,128)(2,1)} %get-tuple-element.195, bf16[2048,2048]{1,0:T(8,128)(2,1)} %get-tuple-element.194, f32[72]{0:T(128)S(1)} %add_rsqrt_fusion, bf16[72,2048]{1,0:T(8,128)(2,1)} %get-tuple-element.193, bf16[8,72,2048]{2,1,0:T(8,128)(2,1)} %get-tuple-element.191, s32[]{:T(128)} %get-tuple-element.192, ...), kind=kOutput, calls=%fused_computation.4 | convolution fusion | flops 1209876480 | bytes 18254112 | tf_op jit(solution)/shard_map/while/body/eval_jaxpr/cond/branch_1_fun/dot_general | solution.py:35
  477.2 1.7 copy.30
  481.3 6.0 collective-permute-done
  487.3 12.8 %conditional.2 = (bf16[72,2048]{1,0:T(8,128)(2,1)}, bf16[1,72,2048]{2,1,0:T(8,128)(2,1)}) conditional(s32[]{:T(128)} %convert_element_type.108, () %tuple.53, (pred[]{:T(512)}, bf16[8,72,2048]{2,1,0:T(8,128)(2,1)}, s32[]{:T(128)}, bf16[72,2048]{1,0:T(8,128)(2,1)}, bf16[2048,2048]{1,0:T(8,128)(2,1)}, /*index=5*/bf16[2048,2048]{1,0:T(8,128)(2,1)}) %tuple.54), branch_computations={%region_1.1_spmd, %region_2.3_spmd} | conditional | flops 1210466432 | bytes 19434644 | solution.py:63
  488.6 9.8 %fusion = bf16[72,2048]{1,0:T(8,128)(2,1)} fusion(bf16[2048,2048]{1,0:T(8,128)(2,1)} %get-tuple-element.195, bf16[2048,2048]{1,0:T(8,128)(2,1)} %get-tuple-element.194, f32[72]{0:T(128)S(1)} %add_rsqrt_fusion, bf16[72,2048]{1,0:T(8,128)(2,1)} %get-tuple-element.193, bf16[8,72,2048]{2,1,0:T(8,128)(2,1)} %get-tuple-element.191, s32[]{:T(128)} %get-tuple-element.192, ...), kind=kOutput, calls=%fused_computation.4 | convolution fusion | flops 1209876480 | bytes 18254112 | tf_op jit(solution)/shard_map/while/body/eval_jaxpr/cond/branch_1_fun/dot_general | solution.py:35
  498.4 1.7 copy.30
  502.5 6.0 collective-permute-done
  508.4 12.8 %conditional.2 = (bf16[72,2048]{1,0:T(8,128)(2,1)}, bf16[1,72,2048]{2,1,0:T(8,128)(2,1)}) conditional(s32[]{:T(128)} %convert_element_type.108, () %tuple.53, (pred[]{:T(512)}, bf16[8,72,2048]{2,1,0:T(8,128)(2,1)}, s32[]{:T(128)}, bf16[72,2048]{1,0:T(8,128)(2,1)}, bf16[2048,2048]{1,0:T(8,128)(2,1)}, /*index=5*/bf16[2048,2048]{1,0:T(8,128)(2,1)}) %tuple.54), branch_computations={%region_1.1_spmd, %region_2.3_spmd} | conditional | flops 1210466432 | bytes 19434644 | solution.py:63
  509.7 9.8 %fusion = bf16[72,2048]{1,0:T(8,128)(2,1)} fusion(bf16[2048,2048]{1,0:T(8,128)(2,1)} %get-tuple-element.195, bf16[2048,2048]{1,0:T(8,128)(2,1)} %get-tuple-element.194, f32[72]{0:T(128)S(1)} %add_rsqrt_fusion, bf16[72,2048]{1,0:T(8,128)(2,1)} %get-tuple-element.193, bf16[8,72,2048]{2,1,0:T(8,128)(2,1)} %get-tuple-element.191, s32[]{:T(128)} %get-tuple-element.192, ...), kind=kOutput, calls=%fused_computation.4 | convolution fusion | flops 1209876480 | bytes 18254112 | tf_op jit(solution)/shard_map/while/body/eval_jaxpr/cond/branch_1_fun/dot_general | solution.py:35
  519.6 1.7 copy.30
  523.6 6.0 collective-permute-done
  529.6 12.8 %conditional.2 = (bf16[72,2048]{1,0:T(8,128)(2,1)}, bf16[1,72,2048]{2,1,0:T(8,128)(2,1)}) conditional(s32[]{:T(128)} %convert_element_type.108, () %tuple.53, (pred[]{:T(512)}, bf16[8,72,2048]{2,1,0:T(8,128)(2,1)}, s32[]{:T(128)}, bf16[72,2048]{1,0:T(8,128)(2,1)}, bf16[2048,2048]{1,0:T(8,128)(2,1)}, /*index=5*/bf16[2048,2048]{1,0:T(8,128)(2,1)}) %tuple.54), branch_computations={%region_1.1_spmd, %region_2.3_spmd} | conditional | flops 1210466432 | bytes 19434644 | solution.py:63
  530.9 9.8 %fusion = bf16[72,2048]{1,0:T(8,128)(2,1)} fusion(bf16[2048,2048]{1,0:T(8,128)(2,1)} %get-tuple-element.195, bf16[2048,2048]{1,0:T(8,128)(2,1)} %get-tuple-element.194, f32[72]{0:T(128)S(1)} %add_rsqrt_fusion, bf16[72,2048]{1,0:T(8,128)(2,1)} %get-tuple-element.193, bf16[8,72,2048]{2,1,0:T(8,128)(2,1)} %get-tuple-element.191, s32[]{:T(128)} %get-tuple-element.192, ...), kind=kOutput, calls=%fused_computation.4 | convolution fusion | flops 1209876480 | bytes 18254112 | tf_op jit(solution)/shard_map/while/body/eval_jaxpr/cond/branch_1_fun/dot_general | solution.py:35
  540.7 1.7 copy.30
  546.2 1.8 gather_fusion
  550.2 1.9 copy.25
  552.1 3.7 reshape.115
  555.8 1.9 convolution_convert_fusion
  557.7 1.7 fusion.43
  559.9 2.1 collective-permute-start.1
  563.3 2.1 collective-permute-start.3
  565.4 2.1 collective-permute-start.4
  567.5 2.1 collective-permute-start.5
  569.6 2.1 collective-permute-start.6
  572.6 2.1 collective-permute-start.7
  575.8 6.0 collective-permute-done.4
  581.8 6.0 collective-permute-done.5
  587.8 1.7 fusion.36
  590.5 20.7 %all_to_all.15 = bf16[32,2,2048]{2,1,0:T(2,128)(2,1)} all-to-all(bf16[32,2,2048]{2,1,0:T(2,128)(2,1)S(1)} %reshape.120), channel_id=1, replica_groups=mesh['section'=8,'expert'=32] {'expert'}, dimensions={0} | all-to-all | bytes 524288 | tf_op jit(solution)/shard_map/all_to_all | solution.py:101
  611.5 24.6 %all-gather.5.cloned.1.call-done = bf16[256,2,2048]{2,1,0:T(2,128)(2,1)} async-done(((bf16[32,2,2048]{2,1,0:T(2,128)(2,1)}), bf16[256,2,2048]{2,1,0:T(2,128)(2,1)}) %all-gather.5.cloned.1.call-update) | async-done | bytes 2097168 | tf_op jit(solution)/shard_map/all_gather | solution.py:102
  636.0 2.7 reshape.121
  640.2 4.9 multiply_convert_fusion.2
  645.2 36.3 %reduce-scatter.2.cloned.1.call-done = bf16[512,256]{1,0:T(8,128)(2,1)} async-done(((bf16[512,2048]{1,0:T(8,128)(2,1)}), bf16[512,256]{1,0:T(8,128)(2,1)}) %reduce-scatter.2.cloned.1.call-update) | async-done | bytes 262160 | tf_op jit(solution)/shard_map/reduce_scatter | solution.py:113
  683.4 9.3 %all-to-all-start.2 = ((bf16[32,8,2,256]{3,2,1,0:T(2,128)(2,1)}), bf16[32,8,2,256]{3,2,1,0:T(2,128)(2,1)S(1)}, u32[]{:S(2)}, u32[]{:S(2)}) async-start(bf16[32,8,2,256]{3,2,1,0:T(2,128)(2,1)} %bitcast.86), calls=%async_computation.3 | async-start | bytes 524288 | tf_op jit(solution)/shard_map/all_to_all | solution.py:115
  692.9 12.6 %all-to-all-done.2 = bf16[32,8,2,256]{3,2,1,0:T(2,128)(2,1)S(1)} async-done(((bf16[32,8,2,256]{3,2,1,0:T(2,128)(2,1)}), bf16[32,8,2,256]{3,2,1,0:T(2,128)(2,1)S(1)}, u32[]{:S(2)}, u32[]{:S(2)}) %all-to-all-start.2) | async-done | bytes 262176 | tf_op jit(solution)/shard_map/all_to_all | solution.py:115
  705.6 2.1 scatter_custom_fusion
  (126 shorter events, 74.9 us)
Async XLA Ops:
  6.5 633.7 %copy-start = (bf16[1,256,2048]{2,1,0:T(8,128)(2,1)S(1)}, bf16[1,256,2048]{2,1,0:T(8,128)(2,1)}, u32[]{:S(2)}) copy-start(bf16[1,256,2048]{2,1,0:T(8,128)(2,1)} %param.17) | copy-start | bytes 3145732
  11.9 12.3 %copy-start.6 = (s32[144,1]{0,1:T(1,128)S(1)}, s32[144,1]{0,1:T(1,128)}, u32[]{:S(2)}) copy-start(s32[144,1]{0,1:T(1,128)} %param.19) | copy-start | bytes 1732
  11.9 13.1 %copy-start.7 = (s32[144]{0:T(256)S(1)}, s32[144]{0:T(256)}, u32[]{:S(2)}) copy-start(s32[144]{0:T(256)} %param.18) | copy-start | bytes 1732
  11.9 242.3 %all-to-all-start = ((bf16[32,1,64,2048]{3,2,1,0:T(8,128)(2,1)}), bf16[32,1,64,2048]{3,2,1,0:T(8,128)(2,1)}, u32[]{:S(2)}, u32[]{:S(2)}) async-start(bf16[32,1,64,2048]{3,2,1,0:T(8,128)(2,1)} %stack.2), calls=%async_computation | async-start | bytes 16777216 | tf_op jit(solution)/shard_map/all_to_all | solution.py:11
  23.4 230.8 %all-gather.3.cloned.1.call-start = ((), (), s32[]{:S(2)}) async-start(), calls=%async_computation.4 | async-start | bytes 8650752 | tf_op jit(solution)/shard_map/all_gather | solution.py:45
  24.1 611.9 %all-gather.5.cloned.1.call-start = ((), (), s32[]{:S(2)}) async-start(), calls=%async_computation.5 | async-start | bytes 2359296 | tf_op jit(solution)/shard_map/all_gather | solution.py:102
  256.7 5.4 collective-permute-start
  263.6 8.3 %collective-permute-start = (bf16[72,2048]{1,0:T(8,128)(2,1)}, bf16[72,2048]{1,0:T(8,128)(2,1)}, u32[]{:S(2)}, u32[]{:S(2)}) collective-permute-start(bf16[72,2048]{1,0:T(8,128)(2,1)} %get-tuple-element.294), channel_id=1, source_target_pairs={{0,32},{32,64},{64,96},{96,128},{128,160},{160,192},{192,224},{1,3... | collective-permute-start | bytes 884744 | tf_op jit(solution)/shard_map/while/body/eval_jaxpr/ppermute | solution.py:21
  273.4 8.3 %collective-permute-start = (bf16[72,2048]{1,0:T(8,128)(2,1)}, bf16[72,2048]{1,0:T(8,128)(2,1)}, u32[]{:S(2)}, u32[]{:S(2)}) collective-permute-start(bf16[72,2048]{1,0:T(8,128)(2,1)} %get-tuple-element.294), channel_id=1, source_target_pairs={{0,32},{32,64},{64,96},{96,128},{128,160},{160,192},{192,224},{1,3... | collective-permute-start | bytes 884744 | tf_op jit(solution)/shard_map/while/body/eval_jaxpr/ppermute | solution.py:21
  283.2 8.3 %collective-permute-start = (bf16[72,2048]{1,0:T(8,128)(2,1)}, bf16[72,2048]{1,0:T(8,128)(2,1)}, u32[]{:S(2)}, u32[]{:S(2)}) collective-permute-start(bf16[72,2048]{1,0:T(8,128)(2,1)} %get-tuple-element.294), channel_id=1, source_target_pairs={{0,32},{32,64},{64,96},{96,128},{128,160},{160,192},{192,224},{1,3... | collective-permute-start | bytes 884744 | tf_op jit(solution)/shard_map/while/body/eval_jaxpr/ppermute | solution.py:21
  293.1 8.3 %collective-permute-start = (bf16[72,2048]{1,0:T(8,128)(2,1)}, bf16[72,2048]{1,0:T(8,128)(2,1)}, u32[]{:S(2)}, u32[]{:S(2)}) collective-permute-start(bf16[72,2048]{1,0:T(8,128)(2,1)} %get-tuple-element.294), channel_id=1, source_target_pairs={{0,32},{32,64},{64,96},{96,128},{128,160},{160,192},{192,224},{1,3... | collective-permute-start | bytes 884744 | tf_op jit(solution)/shard_map/while/body/eval_jaxpr/ppermute | solution.py:21
  302.9 8.3 %collective-permute-start = (bf16[72,2048]{1,0:T(8,128)(2,1)}, bf16[72,2048]{1,0:T(8,128)(2,1)}, u32[]{:S(2)}, u32[]{:S(2)}) collective-permute-start(bf16[72,2048]{1,0:T(8,128)(2,1)} %get-tuple-element.294), channel_id=1, source_target_pairs={{0,32},{32,64},{64,96},{96,128},{128,160},{160,192},{192,224},{1,3... | collective-permute-start | bytes 884744 | tf_op jit(solution)/shard_map/while/body/eval_jaxpr/ppermute | solution.py:21
  312.7 68.8 %collective-permute-start = (bf16[72,2048]{1,0:T(8,128)(2,1)}, bf16[72,2048]{1,0:T(8,128)(2,1)}, u32[]{:S(2)}, u32[]{:S(2)}) collective-permute-start(bf16[72,2048]{1,0:T(8,128)(2,1)} %get-tuple-element.294), channel_id=1, source_target_pairs={{0,32},{32,64},{64,96},{96,128},{128,160},{160,192},{192,224},{1,3... | collective-permute-start | bytes 884744 | tf_op jit(solution)/shard_map/while/body/eval_jaxpr/ppermute | solution.py:21
  394.3 8.4 %collective-permute-start = (bf16[72,2048]{1,0:T(8,128)(2,1)}, bf16[72,2048]{1,0:T(8,128)(2,1)}, u32[]{:S(2)}, u32[]{:S(2)}) collective-permute-start(bf16[72,2048]{1,0:T(8,128)(2,1)} %get-tuple-element.294), channel_id=1, source_target_pairs={{0,32},{32,64},{64,96},{96,128},{128,160},{160,192},{192,224},{1,3... | collective-permute-start | bytes 884744 | tf_op jit(solution)/shard_map/while/body/eval_jaxpr/ppermute | solution.py:21
  415.5 8.3 %collective-permute-start = (bf16[72,2048]{1,0:T(8,128)(2,1)}, bf16[72,2048]{1,0:T(8,128)(2,1)}, u32[]{:S(2)}, u32[]{:S(2)}) collective-permute-start(bf16[72,2048]{1,0:T(8,128)(2,1)} %get-tuple-element.294), channel_id=1, source_target_pairs={{0,32},{32,64},{64,96},{96,128},{128,160},{160,192},{192,224},{1,3... | collective-permute-start | bytes 884744 | tf_op jit(solution)/shard_map/while/body/eval_jaxpr/ppermute | solution.py:21
  436.6 8.3 %collective-permute-start = (bf16[72,2048]{1,0:T(8,128)(2,1)}, bf16[72,2048]{1,0:T(8,128)(2,1)}, u32[]{:S(2)}, u32[]{:S(2)}) collective-permute-start(bf16[72,2048]{1,0:T(8,128)(2,1)} %get-tuple-element.294), channel_id=1, source_target_pairs={{0,32},{32,64},{64,96},{96,128},{128,160},{160,192},{192,224},{1,3... | collective-permute-start | bytes 884744 | tf_op jit(solution)/shard_map/while/body/eval_jaxpr/ppermute | solution.py:21
  457.8 8.3 %collective-permute-start = (bf16[72,2048]{1,0:T(8,128)(2,1)}, bf16[72,2048]{1,0:T(8,128)(2,1)}, u32[]{:S(2)}, u32[]{:S(2)}) collective-permute-start(bf16[72,2048]{1,0:T(8,128)(2,1)} %get-tuple-element.294), channel_id=1, source_target_pairs={{0,32},{32,64},{64,96},{96,128},{128,160},{160,192},{192,224},{1,3... | collective-permute-start | bytes 884744 | tf_op jit(solution)/shard_map/while/body/eval_jaxpr/ppermute | solution.py:21
  478.9 8.3 %collective-permute-start = (bf16[72,2048]{1,0:T(8,128)(2,1)}, bf16[72,2048]{1,0:T(8,128)(2,1)}, u32[]{:S(2)}, u32[]{:S(2)}) collective-permute-start(bf16[72,2048]{1,0:T(8,128)(2,1)} %get-tuple-element.294), channel_id=1, source_target_pairs={{0,32},{32,64},{64,96},{96,128},{128,160},{160,192},{192,224},{1,3... | collective-permute-start | bytes 884744 | tf_op jit(solution)/shard_map/while/body/eval_jaxpr/ppermute | solution.py:21
  500.1 8.3 %collective-permute-start = (bf16[72,2048]{1,0:T(8,128)(2,1)}, bf16[72,2048]{1,0:T(8,128)(2,1)}, u32[]{:S(2)}, u32[]{:S(2)}) collective-permute-start(bf16[72,2048]{1,0:T(8,128)(2,1)} %get-tuple-element.294), channel_id=1, source_target_pairs={{0,32},{32,64},{64,96},{96,128},{128,160},{160,192},{192,224},{1,3... | collective-permute-start | bytes 884744 | tf_op jit(solution)/shard_map/while/body/eval_jaxpr/ppermute | solution.py:21
  521.3 8.3 %collective-permute-start = (bf16[72,2048]{1,0:T(8,128)(2,1)}, bf16[72,2048]{1,0:T(8,128)(2,1)}, u32[]{:S(2)}, u32[]{:S(2)}) collective-permute-start(bf16[72,2048]{1,0:T(8,128)(2,1)} %get-tuple-element.294), channel_id=1, source_target_pairs={{0,32},{32,64},{64,96},{96,128},{128,160},{160,192},{192,224},{1,3... | collective-permute-start | bytes 884744 | tf_op jit(solution)/shard_map/while/body/eval_jaxpr/ppermute | solution.py:21
  542.4 3.8 collective-permute-start
  557.7 2.3 copy-start.1
  559.9 9.7 %collective-permute-start.1 = (bf16[136,2048]{1,0:T(8,128)(2,1)S(1)}, bf16[136,2048]{1,0:T(8,128)(2,1)S(1)}, u32[]{:S(2)}, u32[]{:S(2)}) collective-permute-start(bf16[136,2048]{1,0:T(8,128)(2,1)S(1)} %get-tuple-element.231), channel_id=1, source_target_pairs={{224,192},{225,193},{226,194},{227,195},{228,196},{229,197},{230,1... | collective-permute-start | bytes 1671176 | tf_op jit(solution)/shard_map/ppermute | solution.py:96
  562.0 9.7 %collective-permute-start.2 = (bf16[136,2048]{1,0:T(8,128)(2,1)S(1)}, bf16[136,2048]{1,0:T(8,128)(2,1)S(1)}, u32[]{:S(2)}, u32[]{:S(2)}) collective-permute-start(bf16[136,2048]{1,0:T(8,128)(2,1)S(1)} %get-tuple-element.232), channel_id=1, source_target_pairs={{224,160},{225,161},{226,162},{227,163},{228,164},{229,165},{230,1... | collective-permute-start | bytes 1671176 | tf_op jit(solution)/shard_map/ppermute | solution.py:96
  563.3 12.5 %collective-permute-start.3 = (bf16[136,2048]{1,0:T(8,128)(2,1)}, bf16[136,2048]{1,0:T(8,128)(2,1)}, u32[]{:S(2)}, u32[]{:S(2)}) collective-permute-start(bf16[136,2048]{1,0:T(8,128)(2,1)} %get-tuple-element.233), channel_id=1, source_target_pairs={{224,128},{225,129},{226,130},{227,131},{228,132},{229,133},{230,1... | collective-permute-start | bytes 1671176 | tf_op jit(solution)/shard_map/ppermute | solution.py:96
  565.4 16.3 %collective-permute-start.4 = (bf16[136,2048]{1,0:T(8,128)(2,1)}, bf16[136,2048]{1,0:T(8,128)(2,1)}, u32[]{:S(2)}, u32[]{:S(2)}) collective-permute-start(bf16[136,2048]{1,0:T(8,128)(2,1)} %get-tuple-element.234), channel_id=1, source_target_pairs={{224,96},{225,97},{226,98},{227,99},{228,100},{229,101},{230,102},... | collective-permute-start | bytes 1671176 | tf_op jit(solution)/shard_map/ppermute | solution.py:96
  567.5 20.2 %collective-permute-start.5 = (bf16[136,2048]{1,0:T(8,128)(2,1)}, bf16[136,2048]{1,0:T(8,128)(2,1)}, u32[]{:S(2)}, u32[]{:S(2)}) collective-permute-start(bf16[136,2048]{1,0:T(8,128)(2,1)} %get-tuple-element.235), channel_id=1, source_target_pairs={{224,64},{225,65},{226,66},{227,67},{228,68},{229,69},{230,70},{23... | collective-permute-start | bytes 1671176 | tf_op jit(solution)/shard_map/ppermute | solution.py:96
  569.6 2.1 copy-start.4
  569.6 18.1 %collective-permute-start.6 = (bf16[136,2048]{1,0:T(8,128)(2,1)}, bf16[136,2048]{1,0:T(8,128)(2,1)}, u32[]{:S(2)}, u32[]{:S(2)}) collective-permute-start(bf16[136,2048]{1,0:T(8,128)(2,1)} %get-tuple-element.236), channel_id=1, source_target_pairs={{224,32},{225,33},{226,34},{227,35},{228,36},{229,37},{230,38},{23... | collective-permute-start | bytes 1671176 | tf_op jit(solution)/shard_map/ppermute | solution.py:96
  571.7 0.8 copy-start.5
  572.6 15.2 %collective-permute-start.7 = (bf16[136,2048]{1,0:T(8,128)(2,1)}, bf16[136,2048]{1,0:T(8,128)(2,1)}, u32[]{:S(2)}, u32[]{:S(2)}) collective-permute-start(bf16[136,2048]{1,0:T(8,128)(2,1)} %get-tuple-element.230), channel_id=1, source_target_pairs={{224,0},{225,1},{226,2},{227,3},{228,4},{229,5},{230,6},{231,7},{2... | collective-permute-start | bytes 1671176 | tf_op jit(solution)/shard_map/ppermute | solution.py:96
  589.5 0.8 copy-start.2
  611.2 70.3 %reduce-scatter.2.cloned.1.call-start = ((), (), s32[]{:S(2)}) async-start(), calls=%async_computation.6 | async-start | bytes 2359296 | tf_op jit(solution)/shard_map/reduce_scatter | solution.py:113
  645.1 47.7 %copy-start.3 = (bf16[136,2048]{1,0:T(8,128)(2,1)S(1)}, bf16[136,2048]{1,0:T(8,128)(2,1)}, u32[]{:S(2)}) copy-start(bf16[136,2048]{1,0:T(8,128)(2,1)} %copy-done.2) | copy-start | bytes 1671172
  683.4 22.1 %all-to-all-start.2 = ((bf16[32,8,2,256]{3,2,1,0:T(2,128)(2,1)}), bf16[32,8,2,256]{3,2,1,0:T(2,128)(2,1)S(1)}, u32[]{:S(2)}, u32[]{:S(2)}) async-start(bf16[32,8,2,256]{3,2,1,0:T(2,128)(2,1)} %bitcast.86), calls=%async_computation.3 | async-start | bytes 524288 | tf_op jit(solution)/shard_map/all_to_all | solution.py:115
Sparse Core Ops, SparseCore 0:
  26.7 220.2 all-gather.2
  611.4 24.6 all-gather.4
  645.3 36.1 reduce-scatter.1
